TPU v7x, 32 devices: a whole 2x2x4 slice. The times are simulated.
32 devices in a mesh: groups: 2 (over y), bricks: 4 (over z), heads: 4 (over x, core).
Axes of the slice: x: 2, y: 2, z: 4, core: 2. Of those that a mesh axis runs over, the one named last changes fastest.
Arguments:
- voxel_feats: bfloat16 [4096, 1024], P(('groups', 'bricks'), 'heads'), parts along dimension 0, may hold values from -6 to 6
- face_open: int32 [8], P('groups'), parts along dimension 0, may hold values from 0 to 1
- pattern: int32 [8, 4], P('groups'), parts along dimension 0, may hold values from 0 to 1, as said below
- conv_weight: bfloat16 [27, 1024], P(None, 'heads'), may hold values from -1.25 to 1.25
- conv_bias: bfloat16 [1024], P('heads'), may hold values from -0.5 to 0.5
- gain_one: bfloat16 [1024], replicated, may hold values from 0.099609375 to 1.8984375
- query_weight: bfloat16 [1024, 1024], P(None, 'heads'), may hold values from -3 to 3
- key_weight: bfloat16 [1024, 1024], P(None, 'heads'), may hold values from -3 to 3
- value_weight: bfloat16 [1024, 1024], P(None, 'heads'), may hold values from -0.1875 to 0.1875
- out_weight: bfloat16 [1024, 1024], P('heads'), may hold values from -0.1875 to 0.1875
- gain_two: bfloat16 [1024], replicated, may hold values from 0.099609375 to 1.8984375
- up_weight: bfloat16 [1024, 4096], P(None, 'heads'), may hold values from -0.1875 to 0.1875
- down_weight: bfloat16 [4096, 1024], P('heads'), may hold values from -0.09375 to 0.09375
Outputs:
- block_out: bfloat16 [4096, 1024], P(('groups', 'bricks'), 'heads'), parts along dimension 0
There are 2 independent parts, one for each index of `groups`. A program takes and returns all parts, laid end to end along the dimension named above; an argument that names none is the same for every part. Nothing has to cross between parts.
Inputs may be any that keep to these rules, and one draw needn't show every extreme that they name: pattern is 0 or 1; every brick attends to itself; each query brick attends to 3 or more key bricks, and some query brick to all 4.
All inputs are finite; a program needn't handle non-finite values.
Results may differ from a plain program's by a relative error of at most 0.012.
Values may be sent and summed in bfloat16 or wider, within the bound.
No kernel may reach another device: no remote copies, remote signals or barrier semaphores. Data moves between devices by JAX's collectives and lax.ppermute only.
A program may use at most 64 MiB of HBM per device.

v0:
```python
import jax
import jax.numpy as jnp
from jax import lax
from jax.sharding import PartitionSpec as P

EDGE = 8
HEAD_DIM = 64
epsilon = 1e-05


def extended_2(value, sides, width):
    for axis, dim in sides:
        size, length = (lax.axis_size(axis), value.shape[dim])
        up = [(i, (i + 1) % size) for i in range(size - 1)]
        down = [(j, i) for i, j in up]
        last = lax.slice_in_dim(value, length - width, length, axis=dim)
        first = lax.slice_in_dim(value, 0, width, axis=dim)
        before = lax.ppermute(last, axis, up)
        after = lax.ppermute(first, axis, down)
        value = jnp.concatenate([before, value, after], axis=dim)
    return value


def layer_norm(inputs, gain_vec):
    values = inputs.astype(jnp.float32)
    center = values - jnp.mean(values, axis=-1, keepdims=True)
    spread = jnp.mean(center * center, axis=-1, keepdims=True)
    return center * lax.rsqrt(spread + epsilon) * gain_vec.astype(jnp.float32)


def depthwise(brick_vals, lower_face, upper_face, conv_weight, conv_bias):
    brick_count = brick_vals.shape[0]
    edge_len = brick_vals.shape[1]
    channels = brick_vals.shape[3]
    layers = jnp.concatenate([lower_face[:, None], brick_vals, upper_face[:, None]], axis=1)
    layers = layers.reshape(brick_count, edge_len + 2, edge_len, edge_len, channels)
    padded = jnp.pad(layers, ((0, 0), (0, 0), (1, 1), (1, 1), (0, 0)))
    weights = conv_weight.astype(jnp.float32)
    summed = jnp.zeros((brick_count, edge_len, edge_len, edge_len, channels), jnp.float32)
    for step_x in range(3):
        for step_y in range(3):
            for step_z in range(3):
                window = padded[
                    :,
                    step_x : step_x + edge_len,
                    step_y : step_y + edge_len,
                    step_z : step_z + edge_len,
                ]
                summed = summed + weights[step_x * 9 + step_y * 3 + step_z] * window
    return summed.reshape(brick_count * edge_len**3, channels) + conv_bias.astype(jnp.float32)


def shards(
    voxel_feats,
    face_open,
    pattern,
    conv_weight,
    conv_bias,
    gain_one,
    query_weight,
    key_weight,
    value_weight,
    out_weight,
    gain_two,
    up_weight,
    down_weight,
):
    row_count = voxel_feats.shape[0]
    local_width = voxel_feats.shape[1]
    face_rows = EDGE * EDGE
    brick_rows = EDGE * face_rows
    local_bricks = row_count // brick_rows
    brick_total = pattern.shape[0]
    first_brick = lax.axis_index("bricks") * local_bricks
    extended = extended_2(voxel_feats, (("bricks", 0),), face_rows)
    brick_vals = extended[face_rows : face_rows + row_count].astype(jnp.float32)
    brick_vals = brick_vals.reshape(local_bricks, EDGE, face_rows, local_width)
    lower_face = jnp.concatenate(
        [extended[:face_rows].astype(jnp.float32)[None], brick_vals[:-1, EDGE - 1]], axis=0
    )
    upper_face = jnp.concatenate(
        [brick_vals[1:, 0], extended[face_rows + row_count :].astype(jnp.float32)[None]], axis=0
    )
    brick_ids = first_brick + jnp.arange(local_bricks, dtype=jnp.int32)
    lower_open = jnp.where(brick_ids >= 1, jnp.take(face_open, brick_ids), 0)
    upper_open = jnp.where(
        brick_ids + 1 < brick_total,
        jnp.take(face_open, jnp.minimum(brick_ids + 1, brick_total - 1)),
        0,
    )
    lower_face = lower_face * lower_open.astype(jnp.float32)[:, None, None]
    upper_face = upper_face * upper_open.astype(jnp.float32)[:, None, None]
    conv_out = depthwise(brick_vals, lower_face, upper_face, conv_weight, conv_bias)
    stream = (voxel_feats.astype(jnp.float32) + conv_out).astype(jnp.bfloat16)
    stream_full = lax.all_gather(stream, "heads", axis=1, tiled=True)
    normed = layer_norm(stream_full, gain_one).astype(jnp.bfloat16)
    queries = jnp.dot(normed, query_weight, preferred_element_type=jnp.float32).astype(jnp.bfloat16)
    head_count = local_width // HEAD_DIM
    query_heads = queries.reshape(local_bricks, brick_rows, head_count, HEAD_DIM)
    score_scale = HEAD_DIM ** (-0.5)
    start_state = (
        jnp.full((local_bricks, head_count, brick_rows), -1e30, jnp.float32),
        jnp.zeros((local_bricks, head_count, brick_rows), jnp.float32),
        jnp.zeros((local_bricks, brick_rows, head_count, HEAD_DIM), jnp.float32),
    )

    def absorb(state_in, local_id, key_brick, fetch_pair):
        linked = pattern[first_brick + local_id, key_brick]

        def include(state_now):
            row_max, row_mass, weighted = state_now
            key_rows, value_rows = fetch_pair()
            keys_h = key_rows.reshape(brick_rows, head_count, HEAD_DIM)
            values_h = value_rows.reshape(brick_rows, head_count, HEAD_DIM)
            query_one = lax.dynamic_index_in_dim(query_heads, local_id, 0, keepdims=False)
            scores = (
                jnp.einsum("qhd,khd->hqk", query_one, keys_h, preferred_element_type=jnp.float32)
                * score_scale
            )
            max_old = lax.dynamic_index_in_dim(row_max, local_id, 0, keepdims=False)
            mass_old = lax.dynamic_index_in_dim(row_mass, local_id, 0, keepdims=False)
            sum_old = lax.dynamic_index_in_dim(weighted, local_id, 0, keepdims=False)
            max_new = jnp.maximum(max_old, jnp.max(scores, axis=-1))
            factor = jnp.exp(max_old - max_new)
            weights = jnp.exp(scores - max_new[:, :, None])
            mass_new = mass_old * factor + jnp.sum(weights, axis=-1)
            sum_new = sum_old * jnp.transpose(factor)[:, :, None] + jnp.einsum(
                "hqk,khd->qhd",
                weights.astype(jnp.bfloat16),
                values_h,
                preferred_element_type=jnp.float32,
            )
            return (
                lax.dynamic_update_index_in_dim(row_max, max_new, local_id, 0),
                lax.dynamic_update_index_in_dim(row_mass, mass_new, local_id, 0),
                lax.dynamic_update_index_in_dim(weighted, sum_new, local_id, 0),
            )

        return lax.cond(linked > 0, include, lambda state_now: state_now, state_in)

    keys_all = jnp.dot(normed, key_weight, preferred_element_type=jnp.float32).astype(jnp.bfloat16)
    values_all = jnp.dot(normed, value_weight, preferred_element_type=jnp.float32).astype(
        jnp.bfloat16
    )
    key_piece = lax.all_gather(keys_all, "bricks", axis=0, tiled=True)
    value_piece = lax.all_gather(values_all, "bricks", axis=0, tiled=True)
    piece_bricks = key_piece.shape[0] // brick_rows

    def visit(visit_idx, state_now):
        local_id = visit_idx // piece_bricks
        offset = visit_idx % piece_bricks

        def fetch_pair():
            return (
                lax.dynamic_slice_in_dim(key_piece, offset * brick_rows, brick_rows, 0),
                lax.dynamic_slice_in_dim(value_piece, offset * brick_rows, brick_rows, 0),
            )

        return absorb(state_now, local_id, offset, fetch_pair)

    result = lax.fori_loop(0, local_bricks * piece_bricks, visit, start_state)
    row_max, row_mass, weighted = result
    attended = (weighted / jnp.transpose(row_mass, (0, 2, 1))[:, :, :, None]).astype(jnp.bfloat16)
    attended = attended.reshape(row_count, local_width)
    partial_out = jnp.dot(attended, out_weight, preferred_element_type=jnp.float32)
    full_sum = lax.psum(partial_out.astype(jnp.bfloat16), "heads").astype(jnp.float32)
    stream_two_full = (stream_full.astype(jnp.float32) + full_sum).astype(jnp.bfloat16)
    stream_two = lax.dynamic_slice_in_dim(
        stream_two_full, lax.axis_index("heads") * local_width, local_width, 1
    )
    normed_two = layer_norm(stream_two_full, gain_two).astype(jnp.bfloat16)
    hidden = jax.nn.gelu(
        jnp.dot(normed_two, up_weight, preferred_element_type=jnp.float32), approximate=True
    ).astype(jnp.bfloat16)
    lowered = jnp.dot(hidden, down_weight, preferred_element_type=jnp.float32)
    mixed = lax.psum_scatter(
        lowered.astype(jnp.bfloat16), "heads", scatter_dimension=1, tiled=True
    ).astype(jnp.float32)
    return (stream_two.astype(jnp.float32) + mixed).astype(jnp.bfloat16)


def solution(mesh):
    return jax.shard_map(
        shards,
        mesh=mesh,
        in_specs=(
            P(("groups", "bricks"), "heads"),
            P("groups"),
            P("groups", None),
            P(None, "heads"),
            P("heads"),
            P(),
            P(None, "heads"),
            P(None, "heads"),
            P(None, "heads"),
            P("heads", None),
            P(),
            P(None, "heads"),
            P("heads", None),
        ),
        out_specs=P(("groups", "bricks"), "heads"),
        check_vma=False,
    )
```

profile of v0, /device:TPU:0, one launch (start us, length us, event | category | flops | bytes accessed | tf_op | source)
XLA Modules:
  0.0 208.5 jit_solution(12115050096938499187)
XLA Ops:
  8.8 5.6 %collective-permute-start = (bf16[64,256]{1,0:T(8,128)(2,1)S(1)}, bf16[64,256]{1,0:T(8,128)(2,1)S(1)}, u32[]{:S(2)}, u32[]{:S(2)}) collective-permute-start(bf16[64,256]{1,0:T(8,128)(2,1)S(1)} %get-tuple-element.350), channel_id=1, source_target_pairs={{0,4},{4,8},{8,12},{1,5},{5,9},{9,13},{2,6},{6,10},{10,14},{3,7},{... | collective-permute-start | bytes 98312 | tf_op jit(solution)/shard_map/ppermute | solution.py:18
  16.2 1.4 fusion.98
  20.9 1.6 fusion.57
  23.4 17.6 %all-gather.4.cloned.1.call-done = bf16[512,1024]{1,0:T(8,128)(2,1)} async-done(((bf16[512,256]{1,0:T(8,128)(2,1)}), bf16[512,1024]{1,0:T(8,128)(2,1)}) %all-gather.4.cloned.1.call-update) | async-done | bytes 1048592 | tf_op jit(solution)/shard_map/all_gather | solution.py:95
  41.0 1.5 convert_reduce_fusion
  42.5 1.6 fusion.25
  44.2 2.3 %convolution_convert_fusion.4 = bf16[512,256]{1,0:T(8,128)(2,1)} fusion(bf16[1024,256]{1,0:T(8,128)(2,1)} %param.24, bf16[512,1024]{1,0:T(8,128)(2,1)S(1)} %copy-done.1, f32[1024]{0:T(1024)S(1)} %convert_element_type.108, f32[512]{0:T(512)S(1)} %add_rsqrt_fusion.1, f32[512]{0:T(512)S(1)} %broadcast_multiply_fusion.1), kind=kOutput, calls=%fused_computation.61 | convolution fusion | flops 271187968 | bytes 1843200 | tf_op jit(solution)/shard_map/dot_general | solution.py:141
  46.5 2.3 %convolution_convert_fusion.2 = bf16[512,256]{1,0:T(8,128)(2,1)} fusion(bf16[1024,256]{1,0:T(8,128)(2,1)} %param.25, bf16[512,1024]{1,0:T(8,128)(2,1)S(1)} %copy-done.1, f32[1024]{0:T(1024)S(1)} %convert_element_type.108, f32[512]{0:T(512)S(1)} %add_rsqrt_fusion.1, f32[512]{0:T(512)S(1)} %broadcast_multiply_fusion.1), kind=kOutput, calls=%fused_computation.59 | convolution fusion | flops 271187968 | bytes 1843200 | tf_op jit(solution)/shard_map/dot_general | solution.py:142
  48.8 1.7 convolution_convert_fusion.3
  50.6 24.0 %all-gather.6.cloned.1.call-done = bf16[2048,256]{1,0:T(8,128)(2,1)} async-done(((bf16[512,256]{1,0:T(8,128)(2,1)}), bf16[2048,256]{1,0:T(8,128)(2,1)}) %all-gather.6.cloned.1.call-update) | async-done | bytes 1048592 | tf_op jit(solution)/shard_map/all_gather | solution.py:145
  74.5 2.3 %copy.15 = bf16[2048,256]{0,1:T(8,128)(2,1)} copy(bf16[2048,256]{1,0:T(8,128)(2,1)} %all-gather.6.cloned.1.call-done) | data formatting | bytes 2097152 | tf_op jit(solution)/shard_map/while | solution.py:161
  76.8 26.8 %all-gather.8.cloned.1.call-done = bf16[2048,256]{1,0:T(8,128)(2,1)} async-done(((bf16[512,256]{1,0:T(8,128)(2,1)}), bf16[2048,256]{1,0:T(8,128)(2,1)}) %all-gather.8.cloned.1.call-update) | async-done | bytes 1048592 | tf_op jit(solution)/shard_map/all_gather | solution.py:146
  103.6 2.3 %copy.16 = bf16[2048,256]{0,1:T(8,128)(2,1)} copy(bf16[2048,256]{1,0:T(8,128)(2,1)} %all-gather.8.cloned.1.call-done) | data formatting | bytes 2097152 | tf_op jit(solution)/shard_map/while | solution.py:161
  105.9 22.0 %while.21 = (s32[]{:T(128)}, f32[1,4,512]{2,1,0:T(4,128)S(1)}, f32[1,4,512]{2,1,0:T(4,128)S(1)}, f32[1,512,4,64]{1,3,2,0:T(8,128)S(1)}, s32[]{:T(128)}, /*index=...) while((s32[]{:T(128)}, f32[1,4,512]{2,1,0:T(4,128)S(1)}, ...), condition=%wide.region_7.8_spmd, body=%wide.region_2.0_spmd.sunk | while | flops 277094432 | bytes 15589916 | solution.py:161
  107.9 3.5 %conditional.2 = ((f32[1,4,512]{2,1,0:T(4,128)S(1)}, f32[1,4,512]{2,1,0:T(4,128)S(1)}, f32[1,512,4,64]{1,3,2,0:T(8,128)S(1)})) conditional(s32[]{:T(128)} %bitcast.111, (f32[1,4,512]{2,1,0:T(4,128)S(1)}, f32[1,4,512]{2,1,0:T(4,128)S(1)}, f32[1,512,4,64]{1,3,2,0:T(8,128)S(1)}) %tuple.92, (s32[]{:T(128)}, bf16[2048,256]{0,1:T(8,128)(2,1)}, ...), branch_computations={%region_3.3_spmd, %region_4.6_spmd} | conditional | flops 277094400 | bytes 15589458 | solution.py:139
  113.4 3.5 %conditional.2 = ((f32[1,4,512]{2,1,0:T(4,128)S(1)}, f32[1,4,512]{2,1,0:T(4,128)S(1)}, f32[1,512,4,64]{1,3,2,0:T(8,128)S(1)})) conditional(s32[]{:T(128)} %bitcast.111, (f32[1,4,512]{2,1,0:T(4,128)S(1)}, f32[1,4,512]{2,1,0:T(4,128)S(1)}, f32[1,512,4,64]{1,3,2,0:T(8,128)S(1)}) %tuple.92, (s32[]{:T(128)}, bf16[2048,256]{0,1:T(8,128)(2,1)}, ...), branch_computations={%region_3.3_spmd, %region_4.6_spmd} | conditional | flops 277094400 | bytes 15589458 | solution.py:139
  118.9 3.5 %conditional.2 = ((f32[1,4,512]{2,1,0:T(4,128)S(1)}, f32[1,4,512]{2,1,0:T(4,128)S(1)}, f32[1,512,4,64]{1,3,2,0:T(8,128)S(1)})) conditional(s32[]{:T(128)} %bitcast.111, (f32[1,4,512]{2,1,0:T(4,128)S(1)}, f32[1,4,512]{2,1,0:T(4,128)S(1)}, f32[1,512,4,64]{1,3,2,0:T(8,128)S(1)}) %tuple.92, (s32[]{:T(128)}, bf16[2048,256]{0,1:T(8,128)(2,1)}, ...), branch_computations={%region_3.3_spmd, %region_4.6_spmd} | conditional | flops 277094400 | bytes 15589458 | solution.py:139
  124.4 3.5 %conditional.2 = ((f32[1,4,512]{2,1,0:T(4,128)S(1)}, f32[1,4,512]{2,1,0:T(4,128)S(1)}, f32[1,512,4,64]{1,3,2,0:T(8,128)S(1)})) conditional(s32[]{:T(128)} %bitcast.111, (f32[1,4,512]{2,1,0:T(4,128)S(1)}, f32[1,4,512]{2,1,0:T(4,128)S(1)}, f32[1,512,4,64]{1,3,2,0:T(8,128)S(1)}) %tuple.92, (s32[]{:T(128)}, bf16[2048,256]{0,1:T(8,128)(2,1)}, ...), branch_computations={%region_3.3_spmd, %region_4.6_spmd} | conditional | flops 277094400 | bytes 15589458 | solution.py:139
  128.0 2.6 %convolution_convert_fusion.1 = bf16[512,1024]{1,0:T(8,128)(2,1)} fusion(bf16[512,256]{0,1:T(8,128)(2,1)S(1)} %bitcast.116, bf16[256,1024]{1,0:T(8,128)(2,1)} %param.26), kind=kOutput, calls=%fused_computation.58 | convolution fusion | flops 268959744 | bytes 1835008 | tf_op jit(solution)/shard_map/dot_general | solution.py:165
  130.7 35.7 %all-reduce.3.cloned.1.call-done = bf16[512,1024]{1,0:T(8,128)(2,1)} async-done(((bf16[512,1024]{1,0:T(8,128)(2,1)}), bf16[512,1024]{1,0:T(8,128)(2,1)}) %all-reduce.3.cloned.1.call-update) | async-done | bytes 1048592 | tf_op jit(solution)/shard_map/psum | solution.py:166
  166.4 1.6 convert_reduce_fusion.1
  169.4 5.4 %convolution_convert_fusion = bf16[512,1024]{1,0:T(8,128)(2,1)} fusion(bf16[1024,1024]{1,0:T(8,128)(2,1)S(1)} %copy-done, bf16[1024,1024]{1,0:T(8,128)(2,1)} %param.28, bf16[512,1024]{1,0:T(8,128)(2,1)} %copy-done.3, f32[1024]{0:T(1024)S(1)} %convert_element_type.119, f32[512]{0:T(512)S(1)} %add_rsqrt_fusion, f32[512]{0:T(512)S(1)} %broadcast_multiply_fusion), kind=kOutput, calls=%fused_computation.57 | convolution fusion | flops 2155347968 | bytes 6299648 | tf_op jit(solution)/shard_map/dot_general | solution.py:175
  174.8 25.4 %reduce-scatter.2.cloned.1.call-done = bf16[512,256]{1,0:T(8,128)(2,1)} async-done(((bf16[512,1024]{1,0:T(8,128)(2,1)}), bf16[512,256]{1,0:T(8,128)(2,1)}) %reduce-scatter.2.cloned.1.call-update) | async-done | bytes 262160 | tf_op jit(solution)/shard_map/reduce_scatter | solution.py:176
  200.2 1.8 add_convert_fusion
  (75 shorter events, 27.8 us)
Async XLA Ops:
  6.5 162.8 %copy-start = (bf16[1024,1024]{1,0:T(8,128)(2,1)S(1)}, bf16[1024,1024]{1,0:T(8,128)(2,1)}, u32[]{:S(2)}) copy-start(bf16[1024,1024]{1,0:T(8,128)(2,1)} %param.29) | copy-start | bytes 6291460
  6.5 34.4 %all-gather.4.cloned.1.call-start = ((), (), s32[]{:S(2)}) async-start(), calls=%async_computation.1 | async-start | bytes 1310720 | tf_op jit(solution)/shard_map/all_gather | solution.py:95
  7.5 13.1 %collective-permute-start.1 = (bf16[64,256]{1,0:T(8,128)(2,1)S(1)}, bf16[64,256]{1,0:T(8,128)(2,1)S(1)}, u32[]{:S(2)}, u32[]{:S(2)}) collective-permute-start(bf16[64,256]{1,0:T(8,128)(2,1)S(1)} %get-tuple-element.351), channel_id=1, source_target_pairs={{4,0},{8,4},{12,8},{5,1},{9,5},{13,9},{6,2},{10,6},{14,10},{7,3},{... | collective-permute-start | bytes 98312 | tf_op jit(solution)/shard_map/ppermute | solution.py:19
  8.8 11.8 %collective-permute-start = (bf16[64,256]{1,0:T(8,128)(2,1)S(1)}, bf16[64,256]{1,0:T(8,128)(2,1)S(1)}, u32[]{:S(2)}, u32[]{:S(2)}) collective-permute-start(bf16[64,256]{1,0:T(8,128)(2,1)S(1)} %get-tuple-element.350), channel_id=1, source_target_pairs={{0,4},{4,8},{8,12},{1,5},{5,9},{9,13},{2,6},{6,10},{10,14},{3,7},{... | collective-permute-start | bytes 98312 | tf_op jit(solution)/shard_map/ppermute | solution.py:18
  20.9 1.6 copy-start.4
  20.9 2.5 %copy-start.5 = (bf16[1024]{0:T(1024)(128)(2,1)S(1)}, bf16[1024]{0:T(1024)(128)(2,1)}, u32[]{:S(2)}) copy-start(bf16[1024]{0:T(1024)(128)(2,1)} %param.22) | copy-start | bytes 6148
  23.3 51.2 %all-gather.6.cloned.1.call-start = ((), (), s32[]{:S(2)}) async-start(), calls=%async_computation.2 | async-start | bytes 1310720 | tf_op jit(solution)/shard_map/all_gather | solution.py:145
  41.0 3.2 %copy-start.1 = (bf16[512,1024]{1,0:T(8,128)(2,1)S(1)}, bf16[512,1024]{1,0:T(8,128)(2,1)}, u32[]{:S(2)}) copy-start(bf16[512,1024]{1,0:T(8,128)(2,1)} %all-gather.4.cloned.1.call-done) | copy-start | bytes 3145732
  46.4 57.1 %all-gather.8.cloned.1.call-start = ((), (), s32[]{:S(2)}) async-start(), calls=%async_computation.3 | async-start | bytes 1310720 | tf_op jit(solution)/shard_map/all_gather | solution.py:146
  48.8 117.6 %all-reduce.3.cloned.1.call-start = ((), (), s32[]{:S(2)}) async-start(), calls=%async_computation.4 | async-start | bytes 2097152 | tf_op jit(solution)/shard_map/psum | solution.py:166
  127.9 2.7 %copy-start.6 = (bf16[1024]{0:T(1024)(128)(2,1)S(1)}, bf16[1024]{0:T(1024)(128)(2,1)}, u32[]{:S(2)}) copy-start(bf16[1024]{0:T(1024)(128)(2,1)} %param.27) | copy-start | bytes 6148
  128.0 38.3 %copy-start.2 = (bf16[512,1024]{1,0:T(8,128)(2,1)S(1)}, bf16[512,1024]{1,0:T(8,128)(2,1)}, u32[]{:S(2)}) copy-start(bf16[512,1024]{1,0:T(8,128)(2,1)} %all-gather.4.cloned.1.call-done) | copy-start | bytes 3145732
  130.6 69.5 %reduce-scatter.2.cloned.1.call-start = ((), (), s32[]{:S(2)}) async-start(), calls=%async_computation.5 | async-start | bytes 1310720 | tf_op jit(solution)/shard_map/reduce_scatter | solution.py:176
  168.0 1.0 copy-start.3
Sparse Core Ops, SparseCore 0:
  23.4 17.5 all-gather.3
  46.6 27.9 all-gather.5
  76.1 27.4 all-gather.7
  130.7 35.5 all-reduce.2
  174.9 25.2 reduce-scatter.1
where the time goes:
time: 209 us; the launch traced here: 208 us
  waiting for transfers between devices  129 us (62%)
  matrix products  21 us (10%)
  local copies, waits for them, and re-layouts  19.2 us (9%)
  between operations  14.6 us (7%)
  other arithmetic  14.3 us (7%)
  starting transfers between devices  7.01 us (3%)
  loops' own time  2.85 us (1%)
    psum x1, waiting for transfers between devices, shards(): lax.psum(partial_out.astype(jnp.bfloat16), 'heads').astype(jnp.float32)  35.7 us
    all_gather x1, waiting for transfers between devices, shards(): value_piece = lax.all_gather(values_all, 'bricks', axis=0, tiled=True)  26.8 us
    reduce_scatter x1, waiting for transfers between devices, shards(): lax.psum_scatter(lowered.astype(jnp.bfloat16), 'heads', scatter_dimension...  25.4 us
    all_gather x1, waiting for transfers between devices, shards(): key_piece = lax.all_gather(keys_all, 'bricks', axis=0, tiled=True)  24 us
    all_gather x1, waiting for transfers between devices, shards(): stream_full = lax.all_gather(stream, 'heads', axis=1, tiled=True)  17.6 us
    ppermute x1, starting transfers between devices, extended_2(): before = lax.ppermute(last, axis, up)  5.56 us
    dot_general x1, matrix products, shards(): lowered = jnp.dot(hidden, down_weight, preferred_element_type=jnp.float32)  5.37 us
    dynamic_slice x4, local copies, waits for them, and re-layouts, absorb(): linked = pattern[first_brick + local_id, key_brick]  5.15 us
  transfers between devices with their start and end apart: 7, of which 5 were waited for; matrix products, arithmetic and copies ran while one was open for 5% of the time, Pallas kernels for 0%

commit v1 on v0

--- a/solution.py
+++ b/solution.py
@@ -142,8 +142,13 @@
     values_all = jnp.dot(normed, value_weight, preferred_element_type=jnp.float32).astype(
         jnp.bfloat16
     )
-    key_piece = lax.all_gather(keys_all, "bricks", axis=0, tiled=True)
-    value_piece = lax.all_gather(values_all, "bricks", axis=0, tiled=True)
+    key_piece, value_piece = jnp.split(
+        lax.all_gather(
+            jnp.concatenate([keys_all, values_all], axis=1), "bricks", axis=0, tiled=True
+        ),
+        [keys_all.shape[1]],
+        axis=1,
+    )
     piece_bricks = key_piece.shape[0] // brick_rows
 
     def visit(visit_idx, state_now):

time: 209 us -> 199 us (0.952)
  waiting for transfers between devices: 129 us -> 122 us
  matrix products: 21 us -> 18.9 us
    all_gather x2 -> x1, waiting for transfers between devices: 50.7 us -> 44.3 us  [shards(): lax.all_gather(jnp.concatenate([keys_all, values_all], axis=1), 'bricks',...]
    while x2 -> x0, local copies, waits for them, and re-layouts: 4.55 us -> none  [shards(): result = lax.fori_loop(0, local_bricks * piece_bricks, visit, start_state)]
    split x0 -> x1, local copies, waits for them, and re-layouts: none -> 3.15 us  [shards(): jnp.split(lax.all_gather(jnp.concatenate([keys_all, values_all], axis=1),...]
  transfers between devices with their start and end apart: 7 -> 6, of which waited for: 5 -> 4; matrix products, arithmetic and copies ran while one was open for 5% -> 3% of each run, Pallas kernels for 0% -> 0%
where the time goes in v1:
time: 199 us; the launch traced here: 198 us
  waiting for transfers between devices  122 us (61%)
  matrix products  18.9 us (9%)
  local copies, waits for them, and re-layouts  17.8 us (9%)
  other arithmetic  15.2 us (8%)
  between operations  14.6 us (7%)
  starting transfers between devices  6.97 us (4%)
  loops' own time  2.62 us (1%)
    all_gather x1, waiting for transfers between devices, shards(): lax.all_gather(jnp.concatenate([keys_all, values_all], axis=1), 'bricks',...  44.3 us
    psum x1, waiting for transfers between devices, shards(): lax.psum(partial_out.astype(jnp.bfloat16), 'heads').astype(jnp.float32)  34.9 us
    reduce_scatter x1, waiting for transfers between devices, shards(): lax.psum_scatter(lowered.astype(jnp.bfloat16), 'heads', scatter_dimension...  25.4 us
    all_gather x1, waiting for transfers between devices, shards(): stream_full = lax.all_gather(stream, 'heads', axis=1, tiled=True)  17.6 us
    ppermute x1, starting transfers between devices, extended_2(): before = lax.ppermute(last, axis, up)  5.56 us
    dot_general x1, matrix products, shards(): lowered = jnp.dot(hidden, down_weight, preferred_element_type=jnp.float32)  5.37 us
    dynamic_slice x4, local copies, waits for them, and re-layouts, absorb(): linked = pattern[first_brick + local_id, key_brick]  5.09 us
    dynamic_slice x4, local copies, waits for them, and re-layouts, fetch_pair(): lax.dynamic_slice_in_dim(value_piece, offset * brick_rows, brick_rows, 0)  4.29 us
  transfers between devices with their start and end apart: 6, of which 4 were waited for; matrix products, arithmetic and copies ran while one was open for 3% of the time, Pallas kernels for 0%

profile of v1, /device:TPU:0, one launch (start us, length us, event | category | flops | bytes accessed | tf_op | source)
XLA Modules:
  0.0 198.4 jit_solution(14664629531475574651)
XLA Ops:
  7.5 1.3 collective-permute-start.1
  8.8 5.6 %collective-permute-start = (bf16[64,256]{1,0:T(8,128)(2,1)S(1)}, bf16[64,256]{1,0:T(8,128)(2,1)S(1)}, u32[]{:S(2)}, u32[]{:S(2)}) collective-permute-start(bf16[64,256]{1,0:T(8,128)(2,1)S(1)} %get-tuple-element.343), channel_id=1, source_target_pairs={{0,4},{4,8},{8,12},{1,5},{5,9},{9,13},{2,6},{6,10},{10,14},{3,7},{... | collective-permute-start | bytes 98312 | tf_op jit(solution)/shard_map/ppermute | solution.py:18
  16.2 1.4 fusion.99
  20.8 1.6 fusion.57
  23.3 17.6 %all-gather.3.cloned.1.call-done = bf16[512,1024]{1,0:T(8,128)(2,1)} async-done(((bf16[512,256]{1,0:T(8,128)(2,1)}), bf16[512,1024]{1,0:T(8,128)(2,1)}) %all-gather.3.cloned.1.call-update) | async-done | bytes 1048592 | tf_op jit(solution)/shard_map/all_gather | solution.py:95
  40.9 1.5 convert_reduce_fusion
  42.4 1.7 fusion.25
  44.1 1.7 convolution_convert_fusion.3
  47.5 1.7 convolution_convert_fusion.2
  49.3 44.3 %all-gather.5.cloned.1.call-done = bf16[2048,512]{0,1:T(8,128)(2,1)} async-done(((bf16[512,512]{0,1:T(8,128)(2,1)}), bf16[2048,512]{0,1:T(8,128)(2,1)}) %all-gather.5.cloned.1.call-update) | async-done | bytes 2097168 | tf_op jit(solution)/shard_map/all_gather | solution.py:146
  93.6 3.2 %fusion.95 = (bf16[2048,256]{0,1:T(8,128)(2,1)}, bf16[2048,256]{0,1:T(8,128)(2,1)}) fusion(bf16[2048,512]{0,1:T(8,128)(2,1)} %all-gather.5.cloned.1.call-done), kind=kLoop, calls=%fused_computation.140 | loop fusion | bytes 4194304 | tf_op jit(solution)/shard_map/split | solution.py:145
  96.8 21.7 %while.21 = (s32[]{:T(128)}, f32[1,4,512]{2,1,0:T(4,128)S(1)}, f32[1,4,512]{2,1,0:T(4,128)S(1)}, f32[1,512,4,64]{1,3,2,0:T(8,128)S(1)}, s32[]{:T(128)}, /*index=...) while((s32[]{:T(128)}, f32[1,4,512]{2,1,0:T(4,128)S(1)}, ...), condition=%wide.region_7.8_spmd, body=%wide.region_2.0_spmd.sunk | while | flops 277094432 | bytes 15589916 | solution.py:166
  96.8 1.3 dynamic_slice.33
  98.7 3.5 %conditional.2 = ((f32[1,4,512]{2,1,0:T(4,128)S(1)}, f32[1,4,512]{2,1,0:T(4,128)S(1)}, f32[1,512,4,64]{1,3,2,0:T(8,128)S(1)})) conditional(s32[]{:T(128)} %bitcast.111, (f32[1,4,512]{2,1,0:T(4,128)S(1)}, f32[1,4,512]{2,1,0:T(4,128)S(1)}, f32[1,512,4,64]{1,3,2,0:T(8,128)S(1)}) %tuple.92, (s32[]{:T(128)}, bf16[2048,256]{0,1:T(8,128)(2,1)}, ...), branch_computations={%region_3.3_spmd, %region_4.6_spmd} | conditional | flops 277094400 | bytes 15589458 | solution.py:139
  102.2 1.3 dynamic_slice.33
  104.1 3.5 %conditional.2 = ((f32[1,4,512]{2,1,0:T(4,128)S(1)}, f32[1,4,512]{2,1,0:T(4,128)S(1)}, f32[1,512,4,64]{1,3,2,0:T(8,128)S(1)})) conditional(s32[]{:T(128)} %bitcast.111, (f32[1,4,512]{2,1,0:T(4,128)S(1)}, f32[1,4,512]{2,1,0:T(4,128)S(1)}, f32[1,512,4,64]{1,3,2,0:T(8,128)S(1)}) %tuple.92, (s32[]{:T(128)}, bf16[2048,256]{0,1:T(8,128)(2,1)}, ...), branch_computations={%region_3.3_spmd, %region_4.6_spmd} | conditional | flops 277094400 | bytes 15589458 | solution.py:139
  109.5 3.5 %conditional.2 = ((f32[1,4,512]{2,1,0:T(4,128)S(1)}, f32[1,4,512]{2,1,0:T(4,128)S(1)}, f32[1,512,4,64]{1,3,2,0:T(8,128)S(1)})) conditional(s32[]{:T(128)} %bitcast.111, (f32[1,4,512]{2,1,0:T(4,128)S(1)}, f32[1,4,512]{2,1,0:T(4,128)S(1)}, f32[1,512,4,64]{1,3,2,0:T(8,128)S(1)}) %tuple.92, (s32[]{:T(128)}, bf16[2048,256]{0,1:T(8,128)(2,1)}, ...), branch_computations={%region_3.3_spmd, %region_4.6_spmd} | conditional | flops 277094400 | bytes 15589458 | solution.py:139
  115.0 3.5 %conditional.2 = ((f32[1,4,512]{2,1,0:T(4,128)S(1)}, f32[1,4,512]{2,1,0:T(4,128)S(1)}, f32[1,512,4,64]{1,3,2,0:T(8,128)S(1)})) conditional(s32[]{:T(128)} %bitcast.111, (f32[1,4,512]{2,1,0:T(4,128)S(1)}, f32[1,4,512]{2,1,0:T(4,128)S(1)}, f32[1,512,4,64]{1,3,2,0:T(8,128)S(1)}) %tuple.92, (s32[]{:T(128)}, bf16[2048,256]{0,1:T(8,128)(2,1)}, ...), branch_computations={%region_3.3_spmd, %region_4.6_spmd} | conditional | flops 277094400 | bytes 15589458 | solution.py:139
  118.6 2.6 %convolution_convert_fusion.1 = bf16[512,1024]{1,0:T(8,128)(2,1)} fusion(bf16[512,256]{0,1:T(8,128)(2,1)S(1)} %bitcast.116, bf16[256,1024]{1,0:T(8,128)(2,1)} %param.26), kind=kOutput, calls=%fused_computation.58 | convolution fusion | flops 268959744 | bytes 1835008 | tf_op jit(solution)/shard_map/dot_general | solution.py:170
  121.3 34.9 %all-reduce.3.cloned.1.call-done = bf16[512,1024]{1,0:T(8,128)(2,1)} async-done(((bf16[512,1024]{1,0:T(8,128)(2,1)}), bf16[512,1024]{1,0:T(8,128)(2,1)}) %all-reduce.3.cloned.1.call-update) | async-done | bytes 1048592 | tf_op jit(solution)/shard_map/psum | solution.py:171
  156.2 1.6 convert_reduce_fusion.1
  159.2 5.4 %convolution_convert_fusion = bf16[512,1024]{1,0:T(8,128)(2,1)} fusion(bf16[1024,1024]{1,0:T(8,128)(2,1)S(1)} %copy-done, bf16[1024,1024]{1,0:T(8,128)(2,1)} %param.28, bf16[512,1024]{1,0:T(8,128)(2,1)} %copy-done.3, f32[1024]{0:T(1024)S(1)} %convert_element_type.119, f32[512]{0:T(512)S(1)} %add_rsqrt_fusion, f32[512]{0:T(512)S(1)} %broadcast_multiply_fusion), kind=kOutput, calls=%fused_computation.57 | convolution fusion | flops 2155347968 | bytes 6299648 | tf_op jit(solution)/shard_map/dot_general | solution.py:180
  164.6 25.4 %reduce-scatter.2.cloned.1.call-done = bf16[512,256]{1,0:T(8,128)(2,1)} async-done(((bf16[512,1024]{1,0:T(8,128)(2,1)}), bf16[512,256]{1,0:T(8,128)(2,1)}) %reduce-scatter.2.cloned.1.call-update) | async-done | bytes 262160 | tf_op jit(solution)/shard_map/reduce_scatter | solution.py:181
  190.0 1.8 add_convert_fusion
  (74 shorter events, 25.4 us)
Async XLA Ops:
  6.5 152.7 %copy-start = (bf16[1024,1024]{1,0:T(8,128)(2,1)S(1)}, bf16[1024,1024]{1,0:T(8,128)(2,1)}, u32[]{:S(2)}) copy-start(bf16[1024,1024]{1,0:T(8,128)(2,1)} %param.29) | copy-start | bytes 6291460
  6.5 34.3 %all-gather.3.cloned.1.call-start = ((), (), s32[]{:S(2)}) async-start(), calls=%async_computation.1 | async-start | bytes 1310720 | tf_op jit(solution)/shard_map/all_gather | solution.py:95
  7.5 13.0 %collective-permute-start.1 = (bf16[64,256]{1,0:T(8,128)(2,1)S(1)}, bf16[64,256]{1,0:T(8,128)(2,1)S(1)}, u32[]{:S(2)}, u32[]{:S(2)}) collective-permute-start(bf16[64,256]{1,0:T(8,128)(2,1)S(1)} %get-tuple-element.344), channel_id=1, source_target_pairs={{4,0},{8,4},{12,8},{5,1},{9,5},{13,9},{6,2},{10,6},{14,10},{7,3},{... | collective-permute-start | bytes 98312 | tf_op jit(solution)/shard_map/ppermute | solution.py:19
  8.8 11.7 %collective-permute-start = (bf16[64,256]{1,0:T(8,128)(2,1)S(1)}, bf16[64,256]{1,0:T(8,128)(2,1)S(1)}, u32[]{:S(2)}, u32[]{:S(2)}) collective-permute-start(bf16[64,256]{1,0:T(8,128)(2,1)S(1)} %get-tuple-element.343), channel_id=1, source_target_pairs={{0,4},{4,8},{8,12},{1,5},{5,9},{9,13},{2,6},{6,10},{10,14},{3,7},{... | collective-permute-start | bytes 98312 | tf_op jit(solution)/shard_map/ppermute | solution.py:18
  20.8 1.6 copy-start.4
  20.8 2.5 %copy-start.5 = (bf16[1024]{0:T(1024)(128)(2,1)S(1)}, bf16[1024]{0:T(1024)(128)(2,1)}, u32[]{:S(2)}) copy-start(bf16[1024]{0:T(1024)(128)(2,1)} %param.22) | copy-start | bytes 6148
  23.2 70.4 %all-gather.5.cloned.1.call-start = ((), (), s32[]{:S(2)}) async-start(), calls=%async_computation.2 | async-start | bytes 2621440 | tf_op jit(solution)/shard_map/all_gather | solution.py:146
  40.9 3.2 %copy-start.1 = (bf16[512,1024]{1,0:T(8,128)(2,1)S(1)}, bf16[512,1024]{1,0:T(8,128)(2,1)}, u32[]{:S(2)}) copy-start(bf16[512,1024]{1,0:T(8,128)(2,1)} %all-gather.3.cloned.1.call-done) | copy-start | bytes 3145732
  42.4 3.5 %copy-start.7 = (bf16[1024,256]{1,0:T(8,128)(2,1)S(1)}, bf16[1024,256]{1,0:T(8,128)(2,1)}, u32[]{:S(2)}) copy-start(bf16[1024,256]{1,0:T(8,128)(2,1)} %param.24) | copy-start | bytes 1572868
  47.5 108.7 %all-reduce.3.cloned.1.call-start = ((), (), s32[]{:S(2)}) async-start(), calls=%async_computation.3 | async-start | bytes 2097152 | tf_op jit(solution)/shard_map/psum | solution.py:171
  118.5 2.8 %copy-start.6 = (bf16[1024]{0:T(1024)(128)(2,1)S(1)}, bf16[1024]{0:T(1024)(128)(2,1)}, u32[]{:S(2)}) copy-start(bf16[1024]{0:T(1024)(128)(2,1)} %param.27) | copy-start | bytes 6148
  118.6 37.6 %copy-start.2 = (bf16[512,1024]{1,0:T(8,128)(2,1)S(1)}, bf16[512,1024]{1,0:T(8,128)(2,1)}, u32[]{:S(2)}) copy-start(bf16[512,1024]{1,0:T(8,128)(2,1)} %all-gather.3.cloned.1.call-done) | copy-start | bytes 3145732
  121.2 68.8 %reduce-scatter.2.cloned.1.call-start = ((), (), s32[]{:S(2)}) async-start(), calls=%async_computation.4 | async-start | bytes 1310720 | tf_op jit(solution)/shard_map/reduce_scatter | solution.py:181
  157.8 1.0 copy-start.3
Sparse Core Ops, SparseCore 0:
  23.3 17.5 all-gather.2
  47.6 45.9 all-gather.4
  121.3 34.8 all-reduce.2
  164.7 25.2 reduce-scatter.1
